TPU v7x, 32 devices: a whole 2x2x4 slice. The times are simulated.
32 devices in a mesh: rows: 16 (over z, y, x), vecs: 2 (over core).
Axes of the slice: x: 2, y: 2, z: 4, core: 2. Of those that a mesh axis runs over, the one named last changes fastest.
Arguments:
- vectors: bfloat16 [8192, 256], P('rows', 'vecs'), may hold values from -6 to 6
- blocks: bfloat16 [64, 32, 128, 128], P('rows'), may hold values from -0.09375 to 0.09375
- scales: float32 [64, 32], P('rows'), may hold values from 0.5 to 1.5
- columns: int32 [64, 32], P('rows'), may hold values from 0 to 63, as said below
- owners: int32 [64], P('rows'), may hold values from 0 to 63, as said below
- center: float32 [1], replicated, may hold values from -0.3 to 0.3
- half_width: float32 [1], replicated, may hold values from 1.5 to 2.5
Outputs:
- filtered: bfloat16 [8192, 256], P('rows', 'vecs')
Inputs may be any that keep to these rules, and one draw needn't show every extreme that they name: `columns`: the block rows of one aligned group of 4 block rows read at most one atom of each aligned group of 4 atoms. owners is a permutation of the atoms; the 4 entries of one aligned group of 4 entries lie in distinct aligned groups of 4 atoms.
All inputs are finite; a program needn't handle non-finite values.
Results may differ from a plain program's by a relative error of at most 0.0054.
Values may be sent and summed in bfloat16 or wider, within the bound.
No kernel may reach another device: no remote copies, remote signals or barrier semaphores. Data moves between devices by JAX's collectives and lax.ppermute only.
A program may use at most 64 MiB of HBM per device.

v0:
```python
import jax
import jax.numpy as jnp
from jax import lax
from jax.sharding import PartitionSpec as P

STEPS = 4


def on_device(vectors, blocks, scales, columns, owners, center, half_width):
    local_rows = blocks.shape[0]
    per_row = blocks.shape[1]
    orbitals = blocks.shape[2]
    group_width = vectors.shape[1]

    def gather_all(panels):
        return lax.all_gather(panels, "rows", axis=0, tiled=True)

    def apply_blocks(panels):
        everything = gather_all(panels)
        operand = jnp.take(everything, columns.reshape(-1), axis=0).reshape(
            local_rows, per_row, orbitals, group_width
        )
        partial_value = jnp.einsum(
            "rkij,rkjv->rkiv", blocks, operand, preferred_element_type=jnp.float32
        )
        return jnp.sum(partial_value * scales[:, :, None, None], axis=1)

    shift = center[0]
    width = half_width[0]
    previous = vectors.reshape(local_rows, orbitals, group_width)
    current = ((apply_blocks(previous) - shift * previous.astype(jnp.float32)) / width).astype(
        jnp.bfloat16
    )
    for step in range(STEPS - 1):
        image = apply_blocks(current)
        upcoming = (
            2.0 * (image - shift * current.astype(jnp.float32)) / width
            - previous.astype(jnp.float32)
        ).astype(jnp.bfloat16)
        previous, current = (current, upcoming)
    placed = jnp.take(gather_all(current), owners, axis=0)
    return placed.reshape(local_rows * orbitals, group_width)


def solution(mesh):
    in_specs = (
        P("rows", "vecs"),
        P("rows", None, None, None),
        P("rows", None),
        P("rows", None),
        P("rows"),
        P(),
        P(),
    )
    out_specs = P("rows", "vecs")
    return jax.shard_map(
        on_device, mesh=mesh, in_specs=in_specs, out_specs=out_specs, check_vma=False
    )
```

profile of v0, /device:TPU:0, one launch (start us, length us, event | category | flops | bytes accessed | tf_op | source)
XLA Modules:
  0.0 369.5 jit_solution(10198902864211018663)
XLA Ops:
  6.5 0.7 all-gather.6.cloned.1.call-update
  7.3 1.0 copy.22
  8.3 0.8 reshape.36
  10.4 63.1 %all-gather.6.cloned.1.call-done = bf16[64,128,128]{2,1,0:T(8,128)(2,1)} async-done(((bf16[4,128,128]{2,1,0:T(8,128)(2,1)}), bf16[64,128,128]{2,1,0:T(8,128)(2,1)}) %all-gather.6.cloned.1.call-update) | async-done | bytes 2097168 | tf_op jit(solution)/shard_map/all_gather | solution.py:16
  73.6 4.6 %gather_fusion.1 = bf16[128,128,128]{2,1,0:T(8,128)(2,1)} fusion(bf16[64,128,128]{2,1,0:T(8,128)(2,1)} %all-gather.6.cloned.1.call-done, s32[1024]{0:T(1024)S(1)} %pad_clamp_fusion.1), kind=kCustom, calls=%fused_computation.clone | custom fusion | bytes 8389120 | tf_op jit(solution)/shard_map/jit(_take)/gather | solution.py:20
  78.2 2.8 broadcast_select_fusion
  81.0 0.7 copy-done
  81.6 3.2 multiply_reduce_fusion.3
  84.8 0.8 copy.23
  85.7 59.5 %all-gather.8.cloned.1.call-done = bf16[64,128,128]{2,1,0:T(8,128)(2,1)} async-done(((bf16[4,128,128]{2,1,0:T(8,128)(2,1)}), bf16[64,128,128]{2,1,0:T(8,128)(2,1)}) %all-gather.8.cloned.1.call-update) | async-done | bytes 2097168 | tf_op jit(solution)/shard_map/all_gather | solution.py:16
  145.2 4.6 %gather_fusion.2 = bf16[128,128,128]{2,1,0:T(8,128)(2,1)} fusion(bf16[64,128,128]{2,1,0:T(8,128)(2,1)} %all-gather.8.cloned.1.call-done, s32[1024]{0:T(1024)S(1)} %pad_clamp_fusion.1), kind=kCustom, calls=%fused_computation.1.clone | custom fusion | bytes 8389120 | tf_op jit(solution)/shard_map/jit(_take)/gather | solution.py:20
  149.8 2.8 broadcast_select_fusion.1
  152.6 0.7 copy-done.1
  153.2 3.1 multiply_reduce_fusion.2
  156.4 0.1 fusion.3
  156.5 0.8 copy.25
  157.3 59.5 %all-gather.10.cloned.1.call-done = bf16[64,128,128]{2,1,0:T(8,128)(2,1)} async-done(((bf16[4,128,128]{2,1,0:T(8,128)(2,1)}), bf16[64,128,128]{2,1,0:T(8,128)(2,1)}) %all-gather.10.cloned.1.call-update) | async-done | bytes 2097168 | tf_op jit(solution)/shard_map/all_gather | solution.py:16
  216.8 4.6 %gather_fusion.3 = bf16[128,128,128]{2,1,0:T(8,128)(2,1)} fusion(bf16[64,128,128]{2,1,0:T(8,128)(2,1)} %all-gather.10.cloned.1.call-done, s32[1024]{0:T(1024)S(1)} %pad_clamp_fusion.1), kind=kCustom, calls=%fused_computation.2.clone | custom fusion | bytes 8389120 | tf_op jit(solution)/shard_map/jit(_take)/gather | solution.py:20
  221.4 2.8 broadcast_select_fusion.2
  224.2 0.7 copy-done.2
  224.8 3.1 multiply_reduce_fusion.1
  228.1 0.8 copy.27
  228.9 0.2 all-gather.14.cloned.1.call-start
  229.1 59.3 %all-gather.12.cloned.1.call-done = bf16[64,128,128]{2,1,0:T(8,128)(2,1)} async-done(((bf16[4,128,128]{2,1,0:T(8,128)(2,1)}), bf16[64,128,128]{2,1,0:T(8,128)(2,1)}) %all-gather.12.cloned.1.call-update) | async-done | bytes 2097168 | tf_op jit(solution)/shard_map/all_gather | solution.py:16
  288.4 4.6 %gather_fusion.4 = bf16[128,128,128]{2,1,0:T(8,128)(2,1)} fusion(bf16[64,128,128]{2,1,0:T(8,128)(2,1)} %all-gather.12.cloned.1.call-done, s32[1024]{0:T(1024)S(1)} %pad_clamp_fusion.1), kind=kCustom, calls=%fused_computation.3.clone | custom fusion | bytes 8389120 | tf_op jit(solution)/shard_map/jit(_take)/gather | solution.py:20
  293.0 2.8 broadcast_select_fusion.3
  295.8 0.7 copy-done.3
  296.4 3.1 multiply_reduce_fusion
  299.7 0.8 copy.29
  300.6 59.4 %all-gather.14.cloned.1.call-done = bf16[64,128,128]{2,1,0:T(8,128)(2,1)} async-done(((bf16[4,128,128]{2,1,0:T(8,128)(2,1)}), bf16[64,128,128]{2,1,0:T(8,128)(2,1)}) %all-gather.14.cloned.1.call-update) | async-done | bytes 2097168 | tf_op jit(solution)/shard_map/all_gather | solution.py:16
  360.0 2.2 gather_fusion
  362.2 0.8 bitcast_select_fusion
  (26 shorter events, 0.5 us)
Async XLA Ops:
  6.5 67.0 %all-gather.6.cloned.1.call-start = ((), (), s32[]{:S(2)}) async-start(), calls=%async_computation | async-start | bytes 2228224 | tf_op jit(solution)/shard_map/all_gather | solution.py:16
  7.3 137.9 %all-gather.8.cloned.1.call-start = ((), (), s32[]{:S(2)}) async-start(), calls=%async_computation.1 | async-start | bytes 2228224 | tf_op jit(solution)/shard_map/all_gather | solution.py:16
  78.2 3.4 copy-start
  78.2 3.4 copy-start.4
  85.6 131.1 %all-gather.10.cloned.1.call-start = ((), (), s32[]{:S(2)}) async-start(), calls=%async_computation.2 | async-start | bytes 2228224 | tf_op jit(solution)/shard_map/all_gather | solution.py:16
  149.8 3.4 copy-start.1
  157.3 131.1 %all-gather.12.cloned.1.call-start = ((), (), s32[]{:S(2)}) async-start(), calls=%async_computation.3 | async-start | bytes 2228224 | tf_op jit(solution)/shard_map/all_gather | solution.py:16
  221.4 3.4 copy-start.2
  228.9 131.1 %all-gather.14.cloned.1.call-start = ((), (), s32[]{:S(2)}) async-start(), calls=%async_computation.4 | async-start | bytes 2228224 | tf_op jit(solution)/shard_map/all_gather | solution.py:16
  293.0 3.4 copy-start.3
  296.4 4.0 %copy-start.5 = (s32[4]{0:T(128)S(1)}, s32[4]{0:T(128)}, u32[]{:S(2)}) copy-start(s32[4]{0:T(128)} %param.13) | copy-start | bytes 52
Sparse Core Ops, SparseCore 0:
  10.1 63.3 all-gather.5
  85.8 59.3 all-gather.7
  157.4 59.3 all-gather.9
  229.0 59.3 all-gather.11
  300.6 59.3 all-gather.13
where the time goes:
time: 370 us; the launch traced here: 369 us
  waiting for transfers between devices  301 us (81%)
  local copies, waits for them, and re-layouts  28.2 us (8%)
  between operations  14.6 us (4%)
  matrix products  12.6 us (3%)
  other arithmetic  12.2 us (3%)
    all_gather x5, waiting for transfers between devices, gather_all(): return lax.all_gather(panels, 'rows', axis=0, tiled=True)  301 us
    gather x4, local copies, waits for them, and re-layouts, apply_blocks(): jnp.take(everything, columns.reshape(-1), axis=0)  18.5 us
    dot_general x4, matrix products, apply_blocks(): jnp.einsum('rkij,rkjv->rkiv', blocks, operand, preferred_element_type=jnp...  12.6 us
    select_n x5, other arithmetic, apply_blocks(): jnp.take(everything, columns.reshape(-1), axis=0)  11.1 us
  transfers between devices with their start and end apart: 5, of which 5 were waited for; matrix products, arithmetic and copies ran while one was open for 1% of the time, Pallas kernels for 0%

commit v1 on v0

--- a/solution.py
+++ b/solution.py
@@ -4,6 +4,19 @@
 from jax.sharding import PartitionSpec as P
 
 STEPS = 4
+
+
+def ring_gather(x, axis, dim):
+    ways = lax.axis_size(axis)
+    up = [(d, (d + 1) % ways) for d in range(ways)]
+    down = [(d, (d - 1) % ways) for d in range(ways)]
+    earlier, later = ([x], [x])
+    for _ in range(ways // 2):
+        earlier.append(lax.ppermute(earlier[-1], axis, up))
+    for _ in range((ways - 1) // 2):
+        later.append(lax.ppermute(later[-1], axis, down))
+    line = jnp.concatenate([*earlier[::-1], *later[1:]], axis=dim)
+    return jnp.roll(line, (lax.axis_index(axis) - ways // 2) * x.shape[dim], axis=dim)
 
 
 def on_device(vectors, blocks, scales, columns, owners, center, half_width):
@@ -13,7 +26,7 @@
     group_width = vectors.shape[1]
 
     def gather_all(panels):
-        return lax.all_gather(panels, "rows", axis=0, tiled=True)
+        return ring_gather(panels, "rows", 0)
 
     def apply_blocks(panels):
         everything = gather_all(panels)

time: 370 us -> 407 us (1.10)
  starting transfers between devices: 0.35 us -> 202 us
  waiting for transfers between devices: 301 us -> 155 us
  between operations: 14.6 us -> 2.23 us
  local copies, waits for them, and re-layouts: 28.2 us -> 19.1 us
    all_gather x5 -> x0, waiting for transfers between devices: 301 us -> none  [gather_all(): return lax.all_gather(panels, 'rows', axis=0, tiled=True)]
    ppermute x0 -> x75, starting transfers between devices: none -> 202 us  [the longest x35 199 us: ring_gather(): later.append(lax.ppermute(later[-1], axis, down))]
    ppermute x0 -> x75, waiting for transfers between devices: none -> 155 us  [the longest x40 153 us: ring_gather(): earlier.append(lax.ppermute(earlier[-1], axis, up))]
    gather x4, local copies, waits for them, and re-layouts: 18.5 us -> 12.3 us  [apply_blocks(): jnp.take(everything, columns.reshape(-1), axis=0)]
  transfers between devices with their start and end apart: 5 -> 75, of which waited for: 5 -> 42; matrix products, arithmetic and copies ran while one was open for 1% -> 1% of each run, Pallas kernels for 0% -> 0%
where the time goes in v1:
time: 407 us
  starting transfers between devices  202 us (50%)
  waiting for transfers between devices  155 us (38%)
  local copies, waits for them, and re-layouts  19.1 us (5%)
  other arithmetic  16.2 us (4%)
  matrix products  12.2 us (3%)
    ppermute x35, starting transfers between devices, ring_gather(): later.append(lax.ppermute(later[-1], axis, down))  199 us
    ppermute x40, waiting for transfers between devices, ring_gather(): earlier.append(lax.ppermute(earlier[-1], axis, up))  153 us
    gather x4, local copies, waits for them, and re-layouts, apply_blocks(): jnp.take(everything, columns.reshape(-1), axis=0)  12.3 us
    dot_general x4, matrix products, apply_blocks(): jnp.einsum('rkij,rkjv->rkiv', blocks, operand, preferred_element_type=jnp...  12.2 us
    select_n x5, other arithmetic, apply_blocks(): jnp.take(everything, columns.reshape(-1), axis=0)  11.1 us
  transfers between devices with their start and end apart: 75, of which 42 were waited for; matrix products, arithmetic and copies ran while one was open for 1% of the time, Pallas kernels for 0%

profile of v1, /device:TPU:0, one launch (start us, length us, event | category | flops | bytes accessed | tf_op | source)
XLA Modules:
  0.0 406.6 jit_solution(13467000095377053787)
XLA Ops:
  2.9 7.8 %collective-permute-done = bf16[4,128,128]{2,1,0:T(8,128)(2,1)S(1)} collective-permute-done((bf16[4,128,128]{2,1,0:T(8,128)(2,1)}, bf16[4,128,128]{2,1,0:T(8,128)(2,1)S(1)}, u32[]{:S(2)}, u32[]{:S(2)}) %collective-permute-start) | collective-permute-done | bytes 131104 | tf_op jit(solution)/shard_map/ppermute | solution.py:15
  19.4 5.8 %collective-permute-start.9 = (bf16[4,128,128]{2,1,0:T(8,128)(2,1)S(1)}, bf16[4,128,128]{2,1,0:T(8,128)(2,1)S(1)}, u32[]{:S(2)}, u32[]{:S(2)}) collective-permute-start(bf16[4,128,128]{2,1,0:T(8,128)(2,1)S(1)} %collective-permute-done.8), channel_id=1, source_target_pairs={{0,30},{2,0},{4,2},{6,4},{8,6},{10,8},{12,10},{14,12},{16,14},{18,... | collective-permute-start | bytes 393224 | tf_op jit(solution)/shard_map/ppermute | solution.py:17
  27.9 5.9 %collective-permute-start.10 = (bf16[4,128,128]{2,1,0:T(8,128)(2,1)S(1)}, bf16[4,128,128]{2,1,0:T(8,128)(2,1)S(1)}, u32[]{:S(2)}, u32[]{:S(2)}) collective-permute-start(bf16[4,128,128]{2,1,0:T(8,128)(2,1)S(1)} %collective-permute-done.9), channel_id=1, source_target_pairs={{0,30},{2,0},{4,2},{6,4},{8,6},{10,8},{12,10},{14,12},{16,14},{18,... | collective-permute-start | bytes 393224 | tf_op jit(solution)/shard_map/ppermute | solution.py:17
  36.6 5.8 %collective-permute-start.11 = (bf16[4,128,128]{2,1,0:T(8,128)(2,1)S(1)}, bf16[4,128,128]{2,1,0:T(8,128)(2,1)S(1)}, u32[]{:S(2)}, u32[]{:S(2)}) collective-permute-start(bf16[4,128,128]{2,1,0:T(8,128)(2,1)S(1)} %collective-permute-done.10), channel_id=1, source_target_pairs={{0,30},{2,0},{4,2},{6,4},{8,6},{10,8},{12,10},{14,12},{16,14},{18,... | collective-permute-start | bytes 393224 | tf_op jit(solution)/shard_map/ppermute | solution.py:17
  46.1 5.6 %collective-permute-start.12 = (bf16[4,128,128]{2,1,0:T(8,128)(2,1)S(1)}, bf16[4,128,128]{2,1,0:T(8,128)(2,1)S(1)}, u32[]{:S(2)}, u32[]{:S(2)}) collective-permute-start(bf16[4,128,128]{2,1,0:T(8,128)(2,1)S(1)} %collective-permute-done.11), channel_id=1, source_target_pairs={{0,30},{2,0},{4,2},{6,4},{8,6},{10,8},{12,10},{14,12},{16,14},{18,... | collective-permute-start | bytes 393224 | tf_op jit(solution)/shard_map/ppermute | solution.py:17
  54.7 6.2 %collective-permute-start.13 = (bf16[4,128,128]{2,1,0:T(8,128)(2,1)S(1)}, bf16[4,128,128]{2,1,0:T(8,128)(2,1)S(1)}, u32[]{:S(2)}, u32[]{:S(2)}) collective-permute-start(bf16[4,128,128]{2,1,0:T(8,128)(2,1)S(1)} %collective-permute-done.12), channel_id=1, source_target_pairs={{0,30},{2,0},{4,2},{6,4},{8,6},{10,8},{12,10},{14,12},{16,14},{18,... | collective-permute-start | bytes 393224 | tf_op jit(solution)/shard_map/ppermute | solution.py:17
  66.7 5.6 %collective-permute-start.14 = (bf16[4,128,128]{2,1,0:T(8,128)(2,1)S(1)}, bf16[4,128,128]{2,1,0:T(8,128)(2,1)S(1)}, u32[]{:S(2)}, u32[]{:S(2)}) collective-permute-start(bf16[4,128,128]{2,1,0:T(8,128)(2,1)S(1)} %collective-permute-done.13), channel_id=1, source_target_pairs={{0,30},{2,0},{4,2},{6,4},{8,6},{10,8},{12,10},{14,12},{16,14},{18,... | collective-permute-start | bytes 393224 | tf_op jit(solution)/shard_map/ppermute | solution.py:17
  85.5 9.0 %collective-permute-done.15 = bf16[4,128,128]{1,2,0:T(8,128)(2,1)S(1)} collective-permute-done((bf16[4,128,128]{1,2,0:T(8,128)(2,1)S(1)}, bf16[4,128,128]{1,2,0:T(8,128)(2,1)S(1)}, u32[]{:S(2)}, u32[]{:S(2)}) %collective-permute-start.15) | collective-permute-done | bytes 131104 | tf_op jit(solution)/shard_map/ppermute | solution.py:15
  103.1 5.6 %collective-permute-start.24 = (bf16[4,128,128]{1,2,0:T(8,128)(2,1)S(1)}, bf16[4,128,128]{1,2,0:T(8,128)(2,1)S(1)}, u32[]{:S(2)}, u32[]{:S(2)}) collective-permute-start(bf16[4,128,128]{1,2,0:T(8,128)(2,1)S(1)} %collective-permute-done.23), channel_id=1, source_target_pairs={{0,30},{2,0},{4,2},{6,4},{8,6},{10,8},{12,10},{14,12},{16,14},{18,... | collective-permute-start | bytes 393224 | tf_op jit(solution)/shard_map/ppermute | solution.py:17
  111.8 5.6 %collective-permute-start.25 = (bf16[4,128,128]{1,2,0:T(8,128)(2,1)S(1)}, bf16[4,128,128]{1,2,0:T(8,128)(2,1)S(1)}, u32[]{:S(2)}, u32[]{:S(2)}) collective-permute-start(bf16[4,128,128]{1,2,0:T(8,128)(2,1)S(1)} %collective-permute-done.24), channel_id=1, source_target_pairs={{0,30},{2,0},{4,2},{6,4},{8,6},{10,8},{12,10},{14,12},{16,14},{18,... | collective-permute-start | bytes 393224 | tf_op jit(solution)/shard_map/ppermute | solution.py:17
  121.5 5.7 %collective-permute-start.26 = (bf16[4,128,128]{1,2,0:T(8,128)(2,1)S(1)}, bf16[4,128,128]{1,2,0:T(8,128)(2,1)S(1)}, u32[]{:S(2)}, u32[]{:S(2)}) collective-permute-start(bf16[4,128,128]{1,2,0:T(8,128)(2,1)S(1)} %collective-permute-done.25), channel_id=1, source_target_pairs={{0,30},{2,0},{4,2},{6,4},{8,6},{10,8},{12,10},{14,12},{16,14},{18,... | collective-permute-start | bytes 393224 | tf_op jit(solution)/shard_map/ppermute | solution.py:17
  130.8 5.6 %collective-permute-start.27 = (bf16[4,128,128]{1,2,0:T(8,128)(2,1)S(1)}, bf16[4,128,128]{1,2,0:T(8,128)(2,1)S(1)}, u32[]{:S(2)}, u32[]{:S(2)}) collective-permute-start(bf16[4,128,128]{1,2,0:T(8,128)(2,1)S(1)} %collective-permute-done.26), channel_id=1, source_target_pairs={{0,30},{2,0},{4,2},{6,4},{8,6},{10,8},{12,10},{14,12},{16,14},{18,... | collective-permute-start | bytes 393224 | tf_op jit(solution)/shard_map/ppermute | solution.py:17
  139.4 5.6 %collective-permute-start.28 = (bf16[4,128,128]{1,2,0:T(8,128)(2,1)S(1)}, bf16[4,128,128]{1,2,0:T(8,128)(2,1)S(1)}, u32[]{:S(2)}, u32[]{:S(2)}) collective-permute-start(bf16[4,128,128]{1,2,0:T(8,128)(2,1)S(1)} %collective-permute-done.27), channel_id=1, source_target_pairs={{0,30},{2,0},{4,2},{6,4},{8,6},{10,8},{12,10},{14,12},{16,14},{18,... | collective-permute-start | bytes 393224 | tf_op jit(solution)/shard_map/ppermute | solution.py:17
  148.0 5.6 %collective-permute-start.29 = (bf16[4,128,128]{1,2,0:T(8,128)(2,1)S(1)}, bf16[4,128,128]{1,2,0:T(8,128)(2,1)S(1)}, u32[]{:S(2)}, u32[]{:S(2)}) collective-permute-start(bf16[4,128,128]{1,2,0:T(8,128)(2,1)S(1)} %collective-permute-done.28), channel_id=1, source_target_pairs={{0,30},{2,0},{4,2},{6,4},{8,6},{10,8},{12,10},{14,12},{16,14},{18,... | collective-permute-start | bytes 393224 | tf_op jit(solution)/shard_map/ppermute | solution.py:17
  168.3 8.7 %collective-permute-done.30 = bf16[4,128,128]{1,2,0:T(8,128)(2,1)S(1)} collective-permute-done((bf16[4,128,128]{1,2,0:T(8,128)(2,1)S(1)}, bf16[4,128,128]{1,2,0:T(8,128)(2,1)S(1)}, u32[]{:S(2)}, u32[]{:S(2)}) %collective-permute-start.30) | collective-permute-done | bytes 131104 | tf_op jit(solution)/shard_map/ppermute | solution.py:15
  185.7 5.6 %collective-permute-start.39 = (bf16[4,128,128]{1,2,0:T(8,128)(2,1)S(1)}, bf16[4,128,128]{1,2,0:T(8,128)(2,1)S(1)}, u32[]{:S(2)}, u32[]{:S(2)}) collective-permute-start(bf16[4,128,128]{1,2,0:T(8,128)(2,1)S(1)} %collective-permute-done.38), channel_id=1, source_target_pairs={{0,30},{2,0},{4,2},{6,4},{8,6},{10,8},{12,10},{14,12},{16,14},{18,... | collective-permute-start | bytes 393224 | tf_op jit(solution)/shard_map/ppermute | solution.py:17
  195.5 5.6 %collective-permute-start.40 = (bf16[4,128,128]{1,2,0:T(8,128)(2,1)S(1)}, bf16[4,128,128]{1,2,0:T(8,128)(2,1)S(1)}, u32[]{:S(2)}, u32[]{:S(2)}) collective-permute-start(bf16[4,128,128]{1,2,0:T(8,128)(2,1)S(1)} %collective-permute-done.39), channel_id=1, source_target_pairs={{0,30},{2,0},{4,2},{6,4},{8,6},{10,8},{12,10},{14,12},{16,14},{18,... | collective-permute-start | bytes 393224 | tf_op jit(solution)/shard_map/ppermute | solution.py:17
  204.7 5.6 %collective-permute-start.41 = (bf16[4,128,128]{1,2,0:T(8,128)(2,1)S(1)}, bf16[4,128,128]{1,2,0:T(8,128)(2,1)S(1)}, u32[]{:S(2)}, u32[]{:S(2)}) collective-permute-start(bf16[4,128,128]{1,2,0:T(8,128)(2,1)S(1)} %collective-permute-done.40), channel_id=1, source_target_pairs={{0,30},{2,0},{4,2},{6,4},{8,6},{10,8},{12,10},{14,12},{16,14},{18,... | collective-permute-start | bytes 393224 | tf_op jit(solution)/shard_map/ppermute | solution.py:17
  213.3 5.6 %collective-permute-start.42 = (bf16[4,128,128]{1,2,0:T(8,128)(2,1)S(1)}, bf16[4,128,128]{1,2,0:T(8,128)(2,1)S(1)}, u32[]{:S(2)}, u32[]{:S(2)}) collective-permute-start(bf16[4,128,128]{1,2,0:T(8,128)(2,1)S(1)} %collective-permute-done.41), channel_id=1, source_target_pairs={{0,30},{2,0},{4,2},{6,4},{8,6},{10,8},{12,10},{14,12},{16,14},{18,... | collective-permute-start | bytes 393224 | tf_op jit(solution)/shard_map/ppermute | solution.py:17
  221.9 5.7 %collective-permute-start.43 = (bf16[4,128,128]{1,2,0:T(8,128)(2,1)S(1)}, bf16[4,128,128]{1,2,0:T(8,128)(2,1)S(1)}, u32[]{:S(2)}, u32[]{:S(2)}) collective-permute-start(bf16[4,128,128]{1,2,0:T(8,128)(2,1)S(1)} %collective-permute-done.42), channel_id=1, source_target_pairs={{0,30},{2,0},{4,2},{6,4},{8,6},{10,8},{12,10},{14,12},{16,14},{18,... | collective-permute-start | bytes 393224 | tf_op jit(solution)/shard_map/ppermute | solution.py:17
  231.3 5.6 %collective-permute-start.44 = (bf16[4,128,128]{1,2,0:T(8,128)(2,1)S(1)}, bf16[4,128,128]{1,2,0:T(8,128)(2,1)S(1)}, u32[]{:S(2)}, u32[]{:S(2)}) collective-permute-start(bf16[4,128,128]{1,2,0:T(8,128)(2,1)S(1)} %collective-permute-done.43), channel_id=1, source_target_pairs={{0,30},{2,0},{4,2},{6,4},{8,6},{10,8},{12,10},{14,12},{16,14},{18,... | collective-permute-start | bytes 393224 | tf_op jit(solution)/shard_map/ppermute | solution.py:17
  250.8 8.8 %collective-permute-done.45 = bf16[4,128,128]{1,2,0:T(8,128)(2,1)S(1)} collective-permute-done((bf16[4,128,128]{1,2,0:T(8,128)(2,1)S(1)}, bf16[4,128,128]{1,2,0:T(8,128)(2,1)S(1)}, u32[]{:S(2)}, u32[]{:S(2)}) %collective-permute-start.45) | collective-permute-done | bytes 131104 | tf_op jit(solution)/shard_map/ppermute | solution.py:15
  269.5 5.6 %collective-permute-start.54 = (bf16[4,128,128]{1,2,0:T(8,128)(2,1)S(1)}, bf16[4,128,128]{1,2,0:T(8,128)(2,1)S(1)}, u32[]{:S(2)}, u32[]{:S(2)}) collective-permute-start(bf16[4,128,128]{1,2,0:T(8,128)(2,1)S(1)} %collective-permute-done.53), channel_id=1, source_target_pairs={{0,30},{2,0},{4,2},{6,4},{8,6},{10,8},{12,10},{14,12},{16,14},{18,... | collective-permute-start | bytes 393224 | tf_op jit(solution)/shard_map/ppermute | solution.py:17
  287.3 5.6 %collective-permute-start.56 = (bf16[4,128,128]{1,2,0:T(8,128)(2,1)S(1)}, bf16[4,128,128]{1,2,0:T(8,128)(2,1)S(1)}, u32[]{:S(2)}, u32[]{:S(2)}) collective-permute-start(bf16[4,128,128]{1,2,0:T(8,128)(2,1)S(1)} %collective-permute-done.55), channel_id=1, source_target_pairs={{0,30},{2,0},{4,2},{6,4},{8,6},{10,8},{12,10},{14,12},{16,14},{18,... | collective-permute-start | bytes 393224 | tf_op jit(solution)/shard_map/ppermute | solution.py:17
  295.9 5.7 %collective-permute-start.57 = (bf16[4,128,128]{1,2,0:T(8,128)(2,1)S(1)}, bf16[4,128,128]{1,2,0:T(8,128)(2,1)S(1)}, u32[]{:S(2)}, u32[]{:S(2)}) collective-permute-start(bf16[4,128,128]{1,2,0:T(8,128)(2,1)S(1)} %collective-permute-done.56), channel_id=1, source_target_pairs={{0,30},{2,0},{4,2},{6,4},{8,6},{10,8},{12,10},{14,12},{16,14},{18,... | collective-permute-start | bytes 393224 | tf_op jit(solution)/shard_map/ppermute | solution.py:17
  313.8 5.7 %collective-permute-start.59 = (bf16[4,128,128]{1,2,0:T(8,128)(2,1)S(1)}, bf16[4,128,128]{1,2,0:T(8,128)(2,1)S(1)}, u32[]{:S(2)}, u32[]{:S(2)}) collective-permute-start(bf16[4,128,128]{1,2,0:T(8,128)(2,1)S(1)} %collective-permute-done.58), channel_id=1, source_target_pairs={{0,30},{2,0},{4,2},{6,4},{8,6},{10,8},{12,10},{14,12},{16,14},{18,... | collective-permute-start | bytes 393224 | tf_op jit(solution)/shard_map/ppermute | solution.py:17
  333.3 9.9 %collective-permute-done.60 = bf16[4,128,128]{1,2,0:T(8,128)(2,1)S(1)} collective-permute-done((bf16[4,128,128]{1,2,0:T(8,128)(2,1)S(1)}, bf16[4,128,128]{1,2,0:T(8,128)(2,1)S(1)}, u32[]{:S(2)}, u32[]{:S(2)}) %collective-permute-start.60) | collective-permute-done | bytes 131104 | tf_op jit(solution)/shard_map/ppermute | solution.py:15
  361.0 5.7 %collective-permute-start.70 = (bf16[4,128,128]{1,2,0:T(8,128)(2,1)S(1)}, bf16[4,128,128]{1,2,0:T(8,128)(2,1)S(1)}, u32[]{:S(2)}, u32[]{:S(2)}) collective-permute-start(bf16[4,128,128]{1,2,0:T(8,128)(2,1)S(1)} %collective-permute-done.69), channel_id=1, source_target_pairs={{0,30},{2,0},{4,2},{6,4},{8,6},{10,8},{12,10},{14,12},{16,14},{18,... | collective-permute-start | bytes 393224 | tf_op jit(solution)/shard_map/ppermute | solution.py:17
  369.6 5.7 %collective-permute-start.71 = (bf16[4,128,128]{1,2,0:T(8,128)(2,1)S(1)}, bf16[4,128,128]{1,2,0:T(8,128)(2,1)S(1)}, u32[]{:S(2)}, u32[]{:S(2)}) collective-permute-start(bf16[4,128,128]{1,2,0:T(8,128)(2,1)S(1)} %collective-permute-done.70), channel_id=1, source_target_pairs={{0,30},{2,0},{4,2},{6,4},{8,6},{10,8},{12,10},{14,12},{16,14},{18,... | collective-permute-start | bytes 393224 | tf_op jit(solution)/shard_map/ppermute | solution.py:17
  378.2 5.7 %collective-permute-start.72 = (bf16[4,128,128]{1,2,0:T(8,128)(2,1)S(1)}, bf16[4,128,128]{1,2,0:T(8,128)(2,1)S(1)}, u32[]{:S(2)}, u32[]{:S(2)}) collective-permute-start(bf16[4,128,128]{1,2,0:T(8,128)(2,1)S(1)} %collective-permute-done.71), channel_id=1, source_target_pairs={{0,30},{2,0},{4,2},{6,4},{8,6},{10,8},{12,10},{14,12},{16,14},{18,... | collective-permute-start | bytes 393224 | tf_op jit(solution)/shard_map/ppermute | solution.py:17
  386.7 5.7 %collective-permute-start.73 = (bf16[4,128,128]{1,2,0:T(8,128)(2,1)S(1)}, bf16[4,128,128]{1,2,0:T(8,128)(2,1)S(1)}, u32[]{:S(2)}, u32[]{:S(2)}) collective-permute-start(bf16[4,128,128]{1,2,0:T(8,128)(2,1)S(1)} %collective-permute-done.72), channel_id=1, source_target_pairs={{0,30},{2,0},{4,2},{6,4},{8,6},{10,8},{12,10},{14,12},{16,14},{18,... | collective-permute-start | bytes 393224 | tf_op jit(solution)/shard_map/ppermute | solution.py:17
  395.4 5.7 %collective-permute-start.74 = (bf16[4,128,128]{1,2,0:T(8,128)(2,1)S(1)}, bf16[4,128,128]{1,2,0:T(8,128)(2,1)S(1)}, u32[]{:S(2)}, u32[]{:S(2)}) collective-permute-start(bf16[4,128,128]{1,2,0:T(8,128)(2,1)S(1)} %collective-permute-done.73), channel_id=1, source_target_pairs={{0,30},{2,0},{4,2},{6,4},{8,6},{10,8},{12,10},{14,12},{16,14},{18,... | collective-permute-start | bytes 393224 | tf_op jit(solution)/shard_map/ppermute | solution.py:17
  (245 shorter events, 206.6 us)
Async XLA Ops:
  0.0 10.7 %collective-permute-start = (bf16[4,128,128]{2,1,0:T(8,128)(2,1)}, bf16[4,128,128]{2,1,0:T(8,128)(2,1)S(1)}, u32[]{:S(2)}, u32[]{:S(2)}) collective-permute-start(bf16[4,128,128]{2,1,0:T(8,128)(2,1)} %bitcast.45), channel_id=1, source_target_pairs={{0,2},{2,4},{4,6},{6,8},{8,10},{10,12},{12,14},{14,16},{16,18},{18... | collective-permute-start | bytes 393224 | tf_op jit(solution)/shard_map/ppermute | solution.py:15
  36.6 9.4 %collective-permute-start.11 = (bf16[4,128,128]{2,1,0:T(8,128)(2,1)S(1)}, bf16[4,128,128]{2,1,0:T(8,128)(2,1)S(1)}, u32[]{:S(2)}, u32[]{:S(2)}) collective-permute-start(bf16[4,128,128]{2,1,0:T(8,128)(2,1)S(1)} %collective-permute-done.10), channel_id=1, source_target_pairs={{0,30},{2,0},{4,2},{6,4},{8,6},{10,8},{12,10},{14,12},{16,14},{18,... | collective-permute-start | bytes 393224 | tf_op jit(solution)/shard_map/ppermute | solution.py:17
  45.3 8.9 %collective-permute-start.5 = (bf16[4,128,128]{2,1,0:T(8,128)(2,1)S(1)}, bf16[4,128,128]{2,1,0:T(8,128)(2,1)S(1)}, u32[]{:S(2)}, u32[]{:S(2)}) collective-permute-start(bf16[4,128,128]{2,1,0:T(8,128)(2,1)S(1)} %collective-permute-done.4), channel_id=1, source_target_pairs={{0,2},{2,4},{4,6},{6,8},{8,10},{10,12},{12,14},{14,16},{16,18},{18... | collective-permute-start | bytes 393224 | tf_op jit(solution)/shard_map/ppermute | solution.py:15
  54.2 10.1 %collective-permute-start.6 = (bf16[4,128,128]{2,1,0:T(8,128)(2,1)S(1)}, bf16[4,128,128]{2,1,0:T(8,128)(2,1)S(1)}, u32[]{:S(2)}, u32[]{:S(2)}) collective-permute-start(bf16[4,128,128]{2,1,0:T(8,128)(2,1)S(1)} %collective-permute-done.5), channel_id=1, source_target_pairs={{0,2},{2,4},{4,6},{6,8},{8,10},{10,12},{12,14},{14,16},{16,18},{18... | collective-permute-start | bytes 393224 | tf_op jit(solution)/shard_map/ppermute | solution.py:15
  54.7 11.9 %collective-permute-start.13 = (bf16[4,128,128]{2,1,0:T(8,128)(2,1)S(1)}, bf16[4,128,128]{2,1,0:T(8,128)(2,1)S(1)}, u32[]{:S(2)}, u32[]{:S(2)}) collective-permute-start(bf16[4,128,128]{2,1,0:T(8,128)(2,1)S(1)} %collective-permute-done.12), channel_id=1, source_target_pairs={{0,30},{2,0},{4,2},{6,4},{8,6},{10,8},{12,10},{14,12},{16,14},{18,... | collective-permute-start | bytes 393224 | tf_op jit(solution)/shard_map/ppermute | solution.py:17
  85.4 9.0 %collective-permute-start.15 = (bf16[4,128,128]{1,2,0:T(8,128)(2,1)S(1)}, bf16[4,128,128]{1,2,0:T(8,128)(2,1)S(1)}, u32[]{:S(2)}, u32[]{:S(2)}) collective-permute-start(bf16[4,128,128]{1,2,0:T(8,128)(2,1)S(1)} %fusion.7), channel_id=1, source_target_pairs={{0,2},{2,4},{4,6},{6,8},{8,10},{10,12},{12,14},{14,16},{16,18},{18... | collective-permute-start | bytes 393224 | tf_op jit(solution)/shard_map/ppermute | solution.py:15
  111.8 9.7 %collective-permute-start.18 = (bf16[4,128,128]{1,2,0:T(8,128)(2,1)S(1)}, bf16[4,128,128]{1,2,0:T(8,128)(2,1)S(1)}, u32[]{:S(2)}, u32[]{:S(2)}) collective-permute-start(bf16[4,128,128]{1,2,0:T(8,128)(2,1)S(1)} %collective-permute-done.17), channel_id=1, source_target_pairs={{0,2},{2,4},{4,6},{6,8},{8,10},{10,12},{12,14},{14,16},{16,18},{18... | collective-permute-start | bytes 393224 | tf_op jit(solution)/shard_map/ppermute | solution.py:15
  111.8 9.7 %collective-permute-start.25 = (bf16[4,128,128]{1,2,0:T(8,128)(2,1)S(1)}, bf16[4,128,128]{1,2,0:T(8,128)(2,1)S(1)}, u32[]{:S(2)}, u32[]{:S(2)}) collective-permute-start(bf16[4,128,128]{1,2,0:T(8,128)(2,1)S(1)} %collective-permute-done.24), channel_id=1, source_target_pairs={{0,30},{2,0},{4,2},{6,4},{8,6},{10,8},{12,10},{14,12},{16,14},{18,... | collective-permute-start | bytes 393224 | tf_op jit(solution)/shard_map/ppermute | solution.py:17
  121.5 9.3 %collective-permute-start.19 = (bf16[4,128,128]{1,2,0:T(8,128)(2,1)S(1)}, bf16[4,128,128]{1,2,0:T(8,128)(2,1)S(1)}, u32[]{:S(2)}, u32[]{:S(2)}) collective-permute-start(bf16[4,128,128]{1,2,0:T(8,128)(2,1)S(1)} %collective-permute-done.18), channel_id=1, source_target_pairs={{0,2},{2,4},{4,6},{6,8},{8,10},{10,12},{12,14},{14,16},{16,18},{18... | collective-permute-start | bytes 393224 | tf_op jit(solution)/shard_map/ppermute | solution.py:15
  121.5 9.3 %collective-permute-start.26 = (bf16[4,128,128]{1,2,0:T(8,128)(2,1)S(1)}, bf16[4,128,128]{1,2,0:T(8,128)(2,1)S(1)}, u32[]{:S(2)}, u32[]{:S(2)}) collective-permute-start(bf16[4,128,128]{1,2,0:T(8,128)(2,1)S(1)} %collective-permute-done.25), channel_id=1, source_target_pairs={{0,30},{2,0},{4,2},{6,4},{8,6},{10,8},{12,10},{14,12},{16,14},{18,... | collective-permute-start | bytes 393224 | tf_op jit(solution)/shard_map/ppermute | solution.py:17
  148.0 9.4 %collective-permute-start.22 = (bf16[4,128,128]{1,2,0:T(8,128)(2,1)S(1)}, bf16[4,128,128]{1,2,0:T(8,128)(2,1)S(1)}, u32[]{:S(2)}, u32[]{:S(2)}) collective-permute-start(bf16[4,128,128]{1,2,0:T(8,128)(2,1)S(1)} %collective-permute-done.21), channel_id=1, source_target_pairs={{0,2},{2,4},{4,6},{6,8},{8,10},{10,12},{12,14},{14,16},{16,18},{18... | collective-permute-start | bytes 393224 | tf_op jit(solution)/shard_map/ppermute | solution.py:15
  148.0 9.8 %collective-permute-start.29 = (bf16[4,128,128]{1,2,0:T(8,128)(2,1)S(1)}, bf16[4,128,128]{1,2,0:T(8,128)(2,1)S(1)}, u32[]{:S(2)}, u32[]{:S(2)}) collective-permute-start(bf16[4,128,128]{1,2,0:T(8,128)(2,1)S(1)} %collective-permute-done.28), channel_id=1, source_target_pairs={{0,30},{2,0},{4,2},{6,4},{8,6},{10,8},{12,10},{14,12},{16,14},{18,... | collective-permute-start | bytes 393224 | tf_op jit(solution)/shard_map/ppermute | solution.py:17
  168.3 8.7 %collective-permute-start.30 = (bf16[4,128,128]{1,2,0:T(8,128)(2,1)S(1)}, bf16[4,128,128]{1,2,0:T(8,128)(2,1)S(1)}, u32[]{:S(2)}, u32[]{:S(2)}) collective-permute-start(bf16[4,128,128]{1,2,0:T(8,128)(2,1)S(1)} %fusion.8), channel_id=1, source_target_pairs={{0,2},{2,4},{4,6},{6,8},{8,10},{10,12},{12,14},{14,16},{16,18},{18... | collective-permute-start | bytes 393224 | tf_op jit(solution)/shard_map/ppermute | solution.py:15
  185.7 9.8 %collective-permute-start.32 = (bf16[4,128,128]{1,2,0:T(8,128)(2,1)S(1)}, bf16[4,128,128]{1,2,0:T(8,128)(2,1)S(1)}, u32[]{:S(2)}, u32[]{:S(2)}) collective-permute-start(bf16[4,128,128]{1,2,0:T(8,128)(2,1)S(1)} %collective-permute-done.31), channel_id=1, source_target_pairs={{0,2},{2,4},{4,6},{6,8},{8,10},{10,12},{12,14},{14,16},{16,18},{18... | collective-permute-start | bytes 393224 | tf_op jit(solution)/shard_map/ppermute | solution.py:15
  185.7 9.8 %collective-permute-start.39 = (bf16[4,128,128]{1,2,0:T(8,128)(2,1)S(1)}, bf16[4,128,128]{1,2,0:T(8,128)(2,1)S(1)}, u32[]{:S(2)}, u32[]{:S(2)}) collective-permute-start(bf16[4,128,128]{1,2,0:T(8,128)(2,1)S(1)} %collective-permute-done.38), channel_id=1, source_target_pairs={{0,30},{2,0},{4,2},{6,4},{8,6},{10,8},{12,10},{14,12},{16,14},{18,... | collective-permute-start | bytes 393224 | tf_op jit(solution)/shard_map/ppermute | solution.py:17
  195.5 9.2 %collective-permute-start.33 = (bf16[4,128,128]{1,2,0:T(8,128)(2,1)S(1)}, bf16[4,128,128]{1,2,0:T(8,128)(2,1)S(1)}, u32[]{:S(2)}, u32[]{:S(2)}) collective-permute-start(bf16[4,128,128]{1,2,0:T(8,128)(2,1)S(1)} %collective-permute-done.32), channel_id=1, source_target_pairs={{0,2},{2,4},{4,6},{6,8},{8,10},{10,12},{12,14},{14,16},{16,18},{18... | collective-permute-start | bytes 393224 | tf_op jit(solution)/shard_map/ppermute | solution.py:15
  195.5 9.2 %collective-permute-start.40 = (bf16[4,128,128]{1,2,0:T(8,128)(2,1)S(1)}, bf16[4,128,128]{1,2,0:T(8,128)(2,1)S(1)}, u32[]{:S(2)}, u32[]{:S(2)}) collective-permute-start(bf16[4,128,128]{1,2,0:T(8,128)(2,1)S(1)} %collective-permute-done.39), channel_id=1, source_target_pairs={{0,30},{2,0},{4,2},{6,4},{8,6},{10,8},{12,10},{14,12},{16,14},{18,... | collective-permute-start | bytes 393224 | tf_op jit(solution)/shard_map/ppermute | solution.py:17
  221.9 9.4 %collective-permute-start.36 = (bf16[4,128,128]{1,2,0:T(8,128)(2,1)S(1)}, bf16[4,128,128]{1,2,0:T(8,128)(2,1)S(1)}, u32[]{:S(2)}, u32[]{:S(2)}) collective-permute-start(bf16[4,128,128]{1,2,0:T(8,128)(2,1)S(1)} %collective-permute-done.35), channel_id=1, source_target_pairs={{0,2},{2,4},{4,6},{6,8},{8,10},{10,12},{12,14},{14,16},{16,18},{18... | collective-permute-start | bytes 393224 | tf_op jit(solution)/shard_map/ppermute | solution.py:15
  221.9 9.4 %collective-permute-start.43 = (bf16[4,128,128]{1,2,0:T(8,128)(2,1)S(1)}, bf16[4,128,128]{1,2,0:T(8,128)(2,1)S(1)}, u32[]{:S(2)}, u32[]{:S(2)}) collective-permute-start(bf16[4,128,128]{1,2,0:T(8,128)(2,1)S(1)} %collective-permute-done.42), channel_id=1, source_target_pairs={{0,30},{2,0},{4,2},{6,4},{8,6},{10,8},{12,10},{14,12},{16,14},{18,... | collective-permute-start | bytes 393224 | tf_op jit(solution)/shard_map/ppermute | solution.py:17
  231.3 9.0 %collective-permute-start.44 = (bf16[4,128,128]{1,2,0:T(8,128)(2,1)S(1)}, bf16[4,128,128]{1,2,0:T(8,128)(2,1)S(1)}, u32[]{:S(2)}, u32[]{:S(2)}) collective-permute-start(bf16[4,128,128]{1,2,0:T(8,128)(2,1)S(1)} %collective-permute-done.43), channel_id=1, source_target_pairs={{0,30},{2,0},{4,2},{6,4},{8,6},{10,8},{12,10},{14,12},{16,14},{18,... | collective-permute-start | bytes 393224 | tf_op jit(solution)/shard_map/ppermute | solution.py:17
  250.8 8.8 %collective-permute-start.45 = (bf16[4,128,128]{1,2,0:T(8,128)(2,1)S(1)}, bf16[4,128,128]{1,2,0:T(8,128)(2,1)S(1)}, u32[]{:S(2)}, u32[]{:S(2)}) collective-permute-start(bf16[4,128,128]{1,2,0:T(8,128)(2,1)S(1)} %fusion.12), channel_id=1, source_target_pairs={{0,2},{2,4},{4,6},{6,8},{8,10},{10,12},{12,14},{14,16},{16,18},{18... | collective-permute-start | bytes 393224 | tf_op jit(solution)/shard_map/ppermute | solution.py:15
  259.6 9.9 %collective-permute-start.46 = (bf16[4,128,128]{1,2,0:T(8,128)(2,1)S(1)}, bf16[4,128,128]{1,2,0:T(8,128)(2,1)S(1)}, u32[]{:S(2)}, u32[]{:S(2)}) collective-permute-start(bf16[4,128,128]{1,2,0:T(8,128)(2,1)S(1)} %collective-permute-done.45), channel_id=1, source_target_pairs={{0,2},{2,4},{4,6},{6,8},{8,10},{10,12},{12,14},{14,16},{16,18},{18... | collective-permute-start | bytes 393224 | tf_op jit(solution)/shard_map/ppermute | solution.py:15
  259.6 9.9 %collective-permute-start.53 = (bf16[4,128,128]{1,2,0:T(8,128)(2,1)S(1)}, bf16[4,128,128]{1,2,0:T(8,128)(2,1)S(1)}, u32[]{:S(2)}, u32[]{:S(2)}) collective-permute-start(bf16[4,128,128]{1,2,0:T(8,128)(2,1)S(1)} %fusion.12), channel_id=1, source_target_pairs={{0,30},{2,0},{4,2},{6,4},{8,6},{10,8},{12,10},{14,12},{16,14},{18,... | collective-permute-start | bytes 393224 | tf_op jit(solution)/shard_map/ppermute | solution.py:17
  269.5 9.1 %collective-permute-start.47 = (bf16[4,128,128]{1,2,0:T(8,128)(2,1)S(1)}, bf16[4,128,128]{1,2,0:T(8,128)(2,1)S(1)}, u32[]{:S(2)}, u32[]{:S(2)}) collective-permute-start(bf16[4,128,128]{1,2,0:T(8,128)(2,1)S(1)} %collective-permute-done.46), channel_id=1, source_target_pairs={{0,2},{2,4},{4,6},{6,8},{8,10},{10,12},{12,14},{14,16},{16,18},{18... | collective-permute-start | bytes 393224 | tf_op jit(solution)/shard_map/ppermute | solution.py:15
  269.5 9.1 %collective-permute-start.54 = (bf16[4,128,128]{1,2,0:T(8,128)(2,1)S(1)}, bf16[4,128,128]{1,2,0:T(8,128)(2,1)S(1)}, u32[]{:S(2)}, u32[]{:S(2)}) collective-permute-start(bf16[4,128,128]{1,2,0:T(8,128)(2,1)S(1)} %collective-permute-done.53), channel_id=1, source_target_pairs={{0,30},{2,0},{4,2},{6,4},{8,6},{10,8},{12,10},{14,12},{16,14},{18,... | collective-permute-start | bytes 393224 | tf_op jit(solution)/shard_map/ppermute | solution.py:17
  295.8 9.3 %collective-permute-start.50 = (bf16[4,128,128]{1,2,0:T(8,128)(2,1)S(1)}, bf16[4,128,128]{1,2,0:T(8,128)(2,1)S(1)}, u32[]{:S(2)}, u32[]{:S(2)}) collective-permute-start(bf16[4,128,128]{1,2,0:T(8,128)(2,1)S(1)} %collective-permute-done.49), channel_id=1, source_target_pairs={{0,2},{2,4},{4,6},{6,8},{8,10},{10,12},{12,14},{14,16},{16,18},{18... | collective-permute-start | bytes 393224 | tf_op jit(solution)/shard_map/ppermute | solution.py:15
  295.9 9.3 %collective-permute-start.57 = (bf16[4,128,128]{1,2,0:T(8,128)(2,1)S(1)}, bf16[4,128,128]{1,2,0:T(8,128)(2,1)S(1)}, u32[]{:S(2)}, u32[]{:S(2)}) collective-permute-start(bf16[4,128,128]{1,2,0:T(8,128)(2,1)S(1)} %collective-permute-done.56), channel_id=1, source_target_pairs={{0,30},{2,0},{4,2},{6,4},{8,6},{10,8},{12,10},{14,12},{16,14},{18,... | collective-permute-start | bytes 393224 | tf_op jit(solution)/shard_map/ppermute | solution.py:17
  313.8 9.0 %collective-permute-start.59 = (bf16[4,128,128]{1,2,0:T(8,128)(2,1)S(1)}, bf16[4,128,128]{1,2,0:T(8,128)(2,1)S(1)}, u32[]{:S(2)}, u32[]{:S(2)}) collective-permute-start(bf16[4,128,128]{1,2,0:T(8,128)(2,1)S(1)} %collective-permute-done.58), channel_id=1, source_target_pairs={{0,30},{2,0},{4,2},{6,4},{8,6},{10,8},{12,10},{14,12},{16,14},{18,... | collective-permute-start | bytes 393224 | tf_op jit(solution)/shard_map/ppermute | solution.py:17
  333.2 10.0 %collective-permute-start.60 = (bf16[4,128,128]{1,2,0:T(8,128)(2,1)S(1)}, bf16[4,128,128]{1,2,0:T(8,128)(2,1)S(1)}, u32[]{:S(2)}, u32[]{:S(2)}) collective-permute-start(bf16[4,128,128]{1,2,0:T(8,128)(2,1)S(1)} %fusion.16), channel_id=1, source_target_pairs={{0,2},{2,4},{4,6},{6,8},{8,10},{10,12},{12,14},{14,16},{16,18},{18... | collective-permute-start | bytes 393224 | tf_op jit(solution)/shard_map/ppermute | solution.py:15
  343.2 9.2 %collective-permute-start.61 = (bf16[4,128,128]{1,2,0:T(8,128)(2,1)S(1)}, bf16[4,128,128]{1,2,0:T(8,128)(2,1)S(1)}, u32[]{:S(2)}, u32[]{:S(2)}) collective-permute-start(bf16[4,128,128]{1,2,0:T(8,128)(2,1)S(1)} %collective-permute-done.60), channel_id=1, source_target_pairs={{0,2},{2,4},{4,6},{6,8},{8,10},{10,12},{12,14},{14,16},{16,18},{18... | collective-permute-start | bytes 393224 | tf_op jit(solution)/shard_map/ppermute | solution.py:15
  343.2 9.2 %collective-permute-start.68 = (bf16[4,128,128]{1,2,0:T(8,128)(2,1)S(1)}, bf16[4,128,128]{1,2,0:T(8,128)(2,1)S(1)}, u32[]{:S(2)}, u32[]{:S(2)}) collective-permute-start(bf16[4,128,128]{1,2,0:T(8,128)(2,1)S(1)} %fusion.16), channel_id=1, source_target_pairs={{0,30},{2,0},{4,2},{6,4},{8,6},{10,8},{12,10},{14,12},{16,14},{18,... | collective-permute-start | bytes 393224 | tf_op jit(solution)/shard_map/ppermute | solution.py:17
  395.4 8.9 %collective-permute-start.74 = (bf16[4,128,128]{1,2,0:T(8,128)(2,1)S(1)}, bf16[4,128,128]{1,2,0:T(8,128)(2,1)S(1)}, u32[]{:S(2)}, u32[]{:S(2)}) collective-permute-start(bf16[4,128,128]{1,2,0:T(8,128)(2,1)S(1)} %collective-permute-done.73), channel_id=1, source_target_pairs={{0,30},{2,0},{4,2},{6,4},{8,6},{10,8},{12,10},{14,12},{16,14},{18,... | collective-permute-start | bytes 393224 | tf_op jit(solution)/shard_map/ppermute | solution.py:17
  (50 other events, 508.4 us)
